TPU v7x, 256 devices: a whole 4x4x8 slice. The times are simulated.
256 devices in a mesh: gx: 32 (over x, z), gy: 8 (over y, core).
Axes of the slice: x: 4, y: 4, z: 8, core: 2. Of those that a mesh axis runs over, the one named last changes fastest.
Arguments:
- field: bfloat16 [3, 1, 48, 256, 1024], P(None, None, None, 'gx', 'gy'), may hold values from -6 to 6
- weight_x: bfloat16 [15, 48, 48], replicated, may hold values from -0.21875 to 0.21875
- weight_y: bfloat16 [15, 48, 48], replicated, may hold values from -0.21875 to 0.21875
- cotangent: bfloat16 [3, 1, 48, 256, 1024], P(None, None, None, 'gx', 'gy'), may hold values from -6 to 6
Outputs:
- output: bfloat16 [3, 1, 48, 256, 1024], P(None, None, None, 'gx', 'gy')
- field_grad: bfloat16 [3, 1, 48, 256, 1024], P(None, None, None, 'gx', 'gy')
- wx_grad: float32 [15, 48, 48], replicated
- wy_grad: float32 [15, 48, 48], replicated
All inputs are finite; a program needn't handle non-finite values.
Results may differ from a plain program's by a relative error of at most 0.0054.
Values may be sent and summed in bfloat16 or wider, within the bound.
No kernel may reach another device: no remote copies, remote signals or barrier semaphores. Data moves between devices by JAX's collectives and lax.ppermute only.
A program may use at most 64 MiB of HBM per device.

v0:
```python
import jax
import jax.numpy as jnp
from jax import lax
from jax.sharding import PartitionSpec as P


def with_halo(cells, sides, width):
    for axis, dim in sides:
        count = lax.axis_size(axis)
        ends = count - 1
        head = lax.slice_in_dim(cells, 0, width, axis=dim)
        tail = lax.slice_in_dim(cells, cells.shape[dim] - width, cells.shape[dim], axis=dim)
        cells = jnp.concatenate(
            [
                lax.ppermute(tail, axis, [(i, (i + 1) % count) for i in range(ends)]),
                cells,
                lax.ppermute(head, axis, [((i + 1) % count, i) for i in range(ends)]),
            ],
            axis=dim,
        )
    return cells


def conv_padded(padded, weight, dim):
    taps = weight.shape[0]
    length = padded.shape[dim] - taps + 1
    total = None
    for tap in range(taps):
        piece = lax.slice_in_dim(padded, tap, tap + length, axis=dim)
        term = jnp.einsum("bzcxy,co->bzoxy", piece, weight[tap], preferred_element_type=jnp.float32)
        total = term if total is None else total + term
    return total


def flipped(weight):
    return jnp.transpose(jnp.flip(weight, 0), (0, 2, 1))


def tap_products(padded, grads, taps, dim):
    length = grads.shape[dim]
    terms = []
    for tap in range(taps):
        piece = lax.slice_in_dim(padded, tap, tap + length, axis=dim)
        terms.append(
            jnp.einsum("bzcxy,bzoxy->co", piece, grads, preferred_element_type=jnp.float32)
        )
    return jnp.stack(terms)


def activate(pre):
    return jax.nn.gelu(pre.astype(jnp.float32)).astype(jnp.bfloat16)


def y_reach(values, half):
    return with_halo(values, (("gy", 4),), half)


def per_device(field, weight_x, weight_y, cotangent):
    taps = weight_x.shape[0]
    half = (taps - 1) // 2
    lines = lax.all_to_all(field, "gx", split_axis=4, concat_axis=3, tiled=True)
    lines_pad = jnp.pad(lines, ((0, 0), (0, 0), (0, 0), (half, half), (0, 0)))
    pre_lines = lax.optimization_barrier(conv_padded(lines_pad, weight_x, 3).astype(jnp.bfloat16))
    act_lines = activate(pre_lines)
    act, pre = (
        lax.all_to_all(act_lines, "gx", split_axis=3, concat_axis=4, tiled=True),
        lax.all_to_all(pre_lines, "gx", split_axis=3, concat_axis=4, tiled=True),
    )
    act_pad = y_reach(act, half)
    output = (field.astype(jnp.float32) + conv_padded(act_pad, weight_y, 4)).astype(jnp.bfloat16)
    grad_pad = y_reach(cotangent, half)
    act_grad = conv_padded(grad_pad, flipped(weight_y), 4)
    _, pull = jax.vjp(jax.nn.gelu, pre.astype(jnp.float32))
    pre_grad = pull(act_grad)[0].astype(jnp.bfloat16)
    wy_term = tap_products(act_pad, cotangent, taps, 4)
    paired = with_halo(jnp.stack((field, pre_grad)), (("gx", 4),), half)
    field_pad = paired[0]
    grad_xpad = paired[1]
    field_grad = (
        cotangent.astype(jnp.float32) + conv_padded(grad_xpad, flipped(weight_x), 3)
    ).astype(jnp.bfloat16)
    wx_term = tap_products(field_pad, pre_grad, taps, 3)
    wx_sum, wy_sum = lax.psum((wx_term, wy_term), ("gx", "gy"))
    count = (
        field.shape[0]
        * field.shape[1]
        * field.shape[3]
        * field.shape[4]
        * lax.axis_size("gx")
        * lax.axis_size("gy")
    )
    factor = 1.0 / jnp.sqrt(jnp.float32(count))
    return (output, field_grad, wx_sum * factor, wy_sum * factor)


def solution(mesh):
    in_specs = (P(None, None, None, "gx", "gy"), P(), P(), P(None, None, None, "gx", "gy"))
    out_specs = (P(None, None, None, "gx", "gy"), P(None, None, None, "gx", "gy"), P(), P())
    return jax.shard_map(
        per_device, mesh=mesh, in_specs=in_specs, out_specs=out_specs, check_vma=False
    )
```

profile of v0, /device:TPU:8, one launch (start us, length us, event | category | flops | bytes accessed | tf_op | source)
XLA Modules:
  0.0 378.1 jit_solution(10416243189057325038)
XLA Ops:
  7.2 1.6 copy.144
  8.8 1.7 reshape.644
  10.5 11.3 %all-to-all-start = ((bf16[32,2,2304]{2,1,0:T(2,128)(2,1)}), bf16[32,2,2304]{2,1,0:T(2,128)(2,1)S(1)}, u32[]{:S(2)}, u32[]{:S(2)}) async-start(bf16[32,2,2304]{2,1,0:T(2,128)(2,1)} %reshape.644), calls=%async_computation | async-start | bytes 589824 | tf_op jit(solution)/shard_map/all_to_all | solution.py:61
  22.1 1.9 collective-permute-start.3
  24.0 2.4 collective-permute-start.2
  28.1 3.9 %collective-permute-done.2 = bf16[3,1,48,8,7]{4,2,3,0,1:T(8,128)(2,1)S(1)} collective-permute-done((bf16[3,1,48,8,7]{4,2,3,0,1:T(8,128)(2,1)S(1)}, bf16[3,1,48,8,7]{4,2,3,0,1:T(8,128)(2,1)S(1)}, u32[]{:S(2)}, u32[]{:S(2)}) %collective-permute-start.2) | collective-permute-done | bytes 16160 | tf_op jit(solution)/shard_map/ppermute | solution.py:15
  35.1 1.1 fusion.6
  36.2 0.8 reshape.645
  43.2 1.7 reshape.646
  44.9 10.0 %all-to-all-start.1 = ((bf16[32,2,2304]{2,1,0:T(2,128)(2,1)}), bf16[32,2,2304]{2,1,0:T(2,128)(2,1)S(1)}, u32[]{:S(2)}, u32[]{:S(2)}) async-start(bf16[32,2,2304]{2,1,0:T(2,128)(2,1)} %reshape.646), calls=%async_computation.1 | async-start | bytes 589824 | tf_op jit(solution)/shard_map/all_to_all | solution.py:66
  54.9 1.0 fusion.5
  55.9 1.0 fusion.4
  56.9 1.0 fusion.3
  58.5 1.7 reshape.648
  60.2 6.9 %all-to-all-done.1 = bf16[32,2,2304]{2,1,0:T(2,128)(2,1)S(1)} async-done(((bf16[32,2,2304]{2,1,0:T(2,128)(2,1)}), bf16[32,2,2304]{2,1,0:T(2,128)(2,1)S(1)}, u32[]{:S(2)}, u32[]{:S(2)}) %all-to-all-start.1) | async-done | bytes 294944 | tf_op jit(solution)/shard_map/all_to_all | solution.py:66
  67.1 4.7 %all-to-all-start.2 = ((bf16[32,2,2304]{2,1,0:T(2,128)(2,1)}), bf16[32,2,2304]{2,1,0:T(2,128)(2,1)S(1)}, u32[]{:S(2)}, u32[]{:S(2)}) async-start(bf16[32,2,2304]{2,1,0:T(2,128)(2,1)} %reshape.648), calls=%async_computation.2 | async-start | bytes 589824 | tf_op jit(solution)/shard_map/all_to_all | solution.py:67
  71.9 1.9 fusion.2
  73.7 0.8 reshape.647
  75.8 0.9 fusion.299
  76.7 1.9 collective-permute-start.1
  78.6 2.4 collective-permute-start
  81.0 1.1 fusion.178
  82.1 1.3 all-to-all-done.2
  83.4 0.8 reshape.649
  84.6 1.3 copy.202
  85.9 1.9 fusion.65
  87.9 3.8 %collective-permute-start.4 = (bf16[2,3,1,48,7,128]{5,3,4,1,2,0:T(8,128)(2,1)S(1)}, bf16[2,3,1,48,7,128]{5,3,4,1,2,0:T(8,128)(2,1)S(1)}, u32[]{:S(2)}, u32[]{:S(2)}) collective-permute-start(bf16[2,3,1,48,7,128]{5,3,4,1,2,0:T(8,128)(2,1)S(1)} %get-tuple-element.20), channel_id=1, source_target_pairs={{0,8},{8,16},{16,24},{24,32},{32,40},{40,48},{48,56},{56,64},{64,7... | collective-permute-start | bytes 1548296 | tf_op jit(solution)/shard_map/ppermute | solution.py:15
  91.7 1.5 collective-permute-start.5
  103.7 0.8 copy.220
  113.8 0.8 copy.221
  114.6 254.6 %all-reduce.4.cloned.1.call-done = (f32[15,48,48]{2,1,0:T(8,128)}, f32[15,48,48]{2,1,0:T(8,128)}) async-done(((f32[15,48,48]{2,1,0:T(8,128)}, f32[15,48,48]{2,1,0:T(8,128)}), (f32[15,48,48]{2,1,0:T(8,128)}, f32[15,48,48]{2,1,0:T(8,128)})) %all-reduce.4.cloned.1.call-update) | async-done | bytes 276496 | tf_op jit(solution)/shard_map/psum | solution.py:83
  369.2 2.0 broadcast_multiply_fusion
  (142 shorter events, 32.3 us)
Async XLA Ops:
  7.2 14.7 %copy-start = (bf16[3,1,48,8,128]{4,3,2,1,0:T(8,128)(2,1)S(1)}, bf16[3,1,48,8,128]{4,3,2,1,0:T(8,128)(2,1)}, u32[]{:S(2)}) copy-start(bf16[3,1,48,8,128]{4,3,2,1,0:T(8,128)(2,1)} %param.7) | copy-start | bytes 884740
  8.8 17.7 %copy-start.9 = (bf16[15,48,48]{2,1,0:T(8,128)(2,1)S(1)}, bf16[15,48,48]{2,1,0:T(8,128)(2,1)}, u32[]{:S(2)}) copy-start(bf16[15,48,48]{2,1,0:T(8,128)(2,1)} %param.6) | copy-start | bytes 207364
  10.5 25.7 %all-to-all-start = ((bf16[32,2,2304]{2,1,0:T(2,128)(2,1)}), bf16[32,2,2304]{2,1,0:T(2,128)(2,1)S(1)}, u32[]{:S(2)}, u32[]{:S(2)}) async-start(bf16[32,2,2304]{2,1,0:T(2,128)(2,1)} %reshape.644), calls=%async_computation | async-start | bytes 589824 | tf_op jit(solution)/shard_map/all_to_all | solution.py:61
  21.8 4.9 %copy-start.8 = (bf16[15,48,48]{2,1,0:T(8,128)(2,1)S(1)}, bf16[15,48,48]{2,1,0:T(8,128)(2,1)}, u32[]{:S(2)}) copy-start(bf16[15,48,48]{2,1,0:T(8,128)(2,1)} %param.5) | copy-start | bytes 207364
  21.9 5.5 %copy-start.2 = (bf16[3,1,48,8,128]{4,3,2,1,0:T(8,128)(2,1)S(1)}, bf16[3,1,48,8,128]{4,3,2,1,0:T(8,128)(2,1)}, u32[]{:S(2)}) copy-start(bf16[3,1,48,8,128]{4,3,2,1,0:T(8,128)(2,1)} %param.4) | copy-start | bytes 884740
  22.1 12.6 %collective-permute-start.3 = (bf16[3,1,48,8,7]{4,2,3,0,1:T(8,128)(2,1)S(1)}, bf16[3,1,48,8,7]{4,2,3,0,1:T(8,128)(2,1)S(1)}, u32[]{:S(2)}, u32[]{:S(2)}) collective-permute-start(bf16[3,1,48,8,7]{4,2,3,0,1:T(8,128)(2,1)S(1)} %get-tuple-element.22), channel_id=1, source_target_pairs={{1,0},{2,1},{3,2},{4,3},{5,4},{6,5},{7,6},{9,8},{10,9},{11,10},{12... | collective-permute-start | bytes 48392 | tf_op jit(solution)/shard_map/ppermute | solution.py:17
  24.0 8.0 %collective-permute-start.2 = (bf16[3,1,48,8,7]{4,2,3,0,1:T(8,128)(2,1)S(1)}, bf16[3,1,48,8,7]{4,2,3,0,1:T(8,128)(2,1)S(1)}, u32[]{:S(2)}, u32[]{:S(2)}) collective-permute-start(bf16[3,1,48,8,7]{4,2,3,0,1:T(8,128)(2,1)S(1)} %get-tuple-element.23), channel_id=1, source_target_pairs={{0,1},{1,2},{2,3},{3,4},{4,5},{5,6},{6,7},{8,9},{9,10},{10,11},{11... | collective-permute-start | bytes 48392 | tf_op jit(solution)/shard_map/ppermute | solution.py:15
  26.5 8.6 %copy-start.12 = (bf16[15,48,48]{1,2,0:T(8,128)(2,1)}, bf16[15,48,48]{1,2,0:T(8,128)(2,1)S(1)}, u32[]{:S(2)}) copy-start(bf16[15,48,48]{1,2,0:T(8,128)(2,1)S(1)} %reverse_bitcast_fusion.1) | copy-start | bytes 207364
  42.4 12.5 %copy-start.5 = (f32[48,3,8,128]{3,0,2,1:T(8,128)S(1)}, f32[48,3,8,128]{3,0,2,1:T(8,128)}, u32[]{:S(2)}) copy-start(f32[48,3,8,128]{3,0,2,1:T(8,128)} %fusion.6) | copy-start | bytes 1769476
  44.9 22.2 %all-to-all-start.1 = ((bf16[32,2,2304]{2,1,0:T(2,128)(2,1)}), bf16[32,2,2304]{2,1,0:T(2,128)(2,1)S(1)}, u32[]{:S(2)}, u32[]{:S(2)}) async-start(bf16[32,2,2304]{2,1,0:T(2,128)(2,1)} %reshape.646), calls=%async_computation.1 | async-start | bytes 589824 | tf_op jit(solution)/shard_map/all_to_all | solution.py:66
  67.1 16.3 %all-to-all-start.2 = ((bf16[32,2,2304]{2,1,0:T(2,128)(2,1)}), bf16[32,2,2304]{2,1,0:T(2,128)(2,1)S(1)}, u32[]{:S(2)}, u32[]{:S(2)}) async-start(bf16[32,2,2304]{2,1,0:T(2,128)(2,1)} %reshape.648), calls=%async_computation.2 | async-start | bytes 589824 | tf_op jit(solution)/shard_map/all_to_all | solution.py:67
  71.8 297.4 %all-reduce.4.cloned.1.call-start = ((), (), s32[]{:S(2)}) async-start(), calls=%async_computation.3 | async-start | bytes 1474560 | tf_op jit(solution)/shard_map/psum | solution.py:83
  74.8 6.2 %copy-start.10 = (bf16[15,48,48]{2,1,0:T(8,128)(2,1)S(1)}, bf16[15,48,48]{2,1,0:T(8,128)(2,1)}, u32[]{:S(2)}) copy-start(bf16[15,48,48]{2,1,0:T(8,128)(2,1)} %param.6) | copy-start | bytes 207364
  75.8 8.4 %copy-start.6 = (bf16[3,48,8,128]{3,1,2,0:T(8,128)(2,1)}, bf16[3,48,8,128]{3,1,2,0:T(8,128)(2,1)S(1)}, u32[]{:S(2)}) copy-start(bf16[3,48,8,128]{3,1,2,0:T(8,128)(2,1)S(1)} %copy.179) | copy-start | bytes 884740
  76.7 19.7 %collective-permute-start.1 = (bf16[3,1,48,8,7]{4,2,3,0,1:T(8,128)(2,1)}, bf16[3,1,48,8,7]{4,2,3,0,1:T(8,128)(2,1)S(1)}, u32[]{:S(2)}, u32[]{:S(2)}) collective-permute-start(bf16[3,1,48,8,7]{4,2,3,0,1:T(8,128)(2,1)} %get-tuple-element.26), channel_id=1, source_target_pairs={{1,0},{2,1},{3,2},{4,3},{5,4},{6,5},{7,6},{9,8},{10,9},{11,10},{12... | collective-permute-start | bytes 48392 | tf_op jit(solution)/shard_map/ppermute | solution.py:17
  78.6 14.6 %collective-permute-start = (bf16[3,1,48,8,7]{4,2,3,0,1:T(8,128)(2,1)}, bf16[3,1,48,8,7]{4,2,3,0,1:T(8,128)(2,1)S(1)}, u32[]{:S(2)}, u32[]{:S(2)}) collective-permute-start(bf16[3,1,48,8,7]{4,2,3,0,1:T(8,128)(2,1)} %get-tuple-element.27), channel_id=1, source_target_pairs={{0,1},{1,2},{2,3},{3,4},{4,5},{5,6},{6,7},{8,9},{9,10},{10,11},{11... | collective-permute-start | bytes 48392 | tf_op jit(solution)/shard_map/ppermute | solution.py:15
  85.9 1.9 copy-start.1
  87.9 17.3 %collective-permute-start.4 = (bf16[2,3,1,48,7,128]{5,3,4,1,2,0:T(8,128)(2,1)S(1)}, bf16[2,3,1,48,7,128]{5,3,4,1,2,0:T(8,128)(2,1)S(1)}, u32[]{:S(2)}, u32[]{:S(2)}) collective-permute-start(bf16[2,3,1,48,7,128]{5,3,4,1,2,0:T(8,128)(2,1)S(1)} %get-tuple-element.20), channel_id=1, source_target_pairs={{0,8},{8,16},{16,24},{24,32},{32,40},{40,48},{48,56},{56,64},{64,7... | collective-permute-start | bytes 1548296 | tf_op jit(solution)/shard_map/ppermute | solution.py:15
  91.7 14.8 %collective-permute-start.5 = (bf16[2,3,1,48,7,128]{5,3,4,1,2,0:T(8,128)(2,1)S(1)}, bf16[2,3,1,48,7,128]{5,3,4,1,2,0:T(8,128)(2,1)S(1)}, u32[]{:S(2)}, u32[]{:S(2)}) collective-permute-start(bf16[2,3,1,48,7,128]{5,3,4,1,2,0:T(8,128)(2,1)S(1)} %get-tuple-element.21), channel_id=1, source_target_pairs={{8,0},{16,8},{24,16},{32,24},{40,32},{48,40},{56,48},{64,56},{72,6... | collective-permute-start | bytes 1548296 | tf_op jit(solution)/shard_map/ppermute | solution.py:17
  94.6 1.1 copy-start.7
  98.9 1.1 copy-start.4
  102.0 1.0 copy-start.3
  105.2 0.7 copy-start.13
  109.3 1.2 copy-start.11
  110.4 0.7 copy-start.14
Sparse Core Ops, SparseCore 0:
  113.7 255.4 all-reduce.3
where the time goes:
time: 379 us; the launch traced here: 378 us
  waiting for transfers between devices  267 us (70%)
  starting transfers between devices  40 us (11%)
  matrix products  33.7 us (9%)
  local copies, waits for them, and re-layouts  19.4 us (5%)
  between operations  15.2 us (4%)
    psum x1, waiting for transfers between devices, per_device(): wx_sum, wy_sum = lax.psum((wx_term, wy_term), ('gx', 'gy'))  255 us
    dot_general x60, matrix products, conv_padded(): jnp.einsum('bzcxy,co->bzoxy', piece, weight[tap], preferred_element_type=...  25.2 us
    unnamed x41, local copies, waits for them, and re-layouts  12.9 us
    all_to_all x1, starting transfers between devices, per_device(): lines = lax.all_to_all(field, 'gx', split_axis=4, concat_axis=3, tiled=True)  11.3 us
    all_to_all x1, starting transfers between devices, per_device(): lax.all_to_all(act_lines, 'gx', split_axis=3, concat_axis=4, tiled=True)  9.97 us
    ppermute x3, starting transfers between devices, with_halo(): lax.ppermute(tail, axis, [(i, (i + 1) % count) for i in range(ends)])  8.62 us
    dot_general x30, matrix products, tap_products(): jnp.einsum('bzcxy,bzoxy->co', piece, grads, preferred_element_type=jnp.fl...  8.47 us
  transfers between devices with their start and end apart: 10, of which 5 were waited for; matrix products, arithmetic and copies ran while one was open for 9% of the time, Pallas kernels for 0%

commit v1 on v0

--- a/solution.py
+++ b/solution.py
@@ -80,7 +80,7 @@
         cotangent.astype(jnp.float32) + conv_padded(grad_xpad, flipped(weight_x), 3)
     ).astype(jnp.bfloat16)
     wx_term = tap_products(field_pad, pre_grad, taps, 3)
-    wx_sum, wy_sum = lax.psum((wx_term, wy_term), ("gx", "gy"))
+    wx_sum, wy_sum = lax.psum(lax.psum((wx_term, wy_term), "gy"), "gx")
     count = (
         field.shape[0]
         * field.shape[1]

time: 379 us -> 342 us (0.902)
  waiting for transfers between devices: 267 us -> 231 us
    psum x1 -> x2, waiting for transfers between devices: 255 us -> 218 us  [per_device(): wx_sum, wy_sum = lax.psum(lax.psum((wx_term, wy_term), 'gy'), 'gx')]
  transfers between devices with their start and end apart: 10 -> 11, of which waited for: 5 -> 6; matrix products, arithmetic and copies ran while one was open for 9% -> 10% of each run, Pallas kernels for 0% -> 0%
where the time goes in v1:
time: 342 us
  waiting for transfers between devices  231 us (68%)
  starting transfers between devices  40 us (12%)
  matrix products  33.7 us (10%)
  local copies, waits for them, and re-layouts  19.4 us (6%)
  between operations  15.2 us (4%)
    psum x2, waiting for transfers between devices, per_device(): wx_sum, wy_sum = lax.psum(lax.psum((wx_term, wy_term), 'gy'), 'gx')  218 us
    dot_general x60, matrix products, conv_padded(): jnp.einsum('bzcxy,co->bzoxy', piece, weight[tap], preferred_element_type=...  25.2 us
    unnamed x41, local copies, waits for them, and re-layouts  12.9 us
    all_to_all x1, starting transfers between devices, per_device(): lines = lax.all_to_all(field, 'gx', split_axis=4, concat_axis=3, tiled=True)  11.3 us
    all_to_all x1, starting transfers between devices, per_device(): lax.all_to_all(act_lines, 'gx', split_axis=3, concat_axis=4, tiled=True)  9.96 us
    ppermute x3, starting transfers between devices, with_halo(): lax.ppermute(tail, axis, [(i, (i + 1) % count) for i in range(ends)])  8.62 us
    dot_general x30, matrix products, tap_products(): jnp.einsum('bzcxy,bzoxy->co', piece, grads, preferred_element_type=jnp.fl...  8.47 us
    all_to_all x1, waiting for transfers between devices, per_device(): lax.all_to_all(act_lines, 'gx', split_axis=3, concat_axis=4, tiled=True)  6.88 us
  transfers between devices with their start and end apart: 11, of which 6 were waited for; matrix products, arithmetic and copies ran while one was open for 10% of the time, Pallas kernels for 0%

profile of v1, /device:TPU:8, one launch (start us, length us, event | category | flops | bytes accessed | tf_op | source)
XLA Modules:
  0.0 341.6 jit_solution(9048228014717731848)
XLA Ops:
  7.2 1.6 copy.144
  8.8 1.7 reshape.644
  10.5 11.3 %all-to-all-start = ((bf16[32,2,2304]{2,1,0:T(2,128)(2,1)}), bf16[32,2,2304]{2,1,0:T(2,128)(2,1)S(1)}, u32[]{:S(2)}, u32[]{:S(2)}) async-start(bf16[32,2,2304]{2,1,0:T(2,128)(2,1)} %reshape.644), calls=%async_computation | async-start | bytes 589824 | tf_op jit(solution)/shard_map/all_to_all | solution.py:61
  22.1 1.9 collective-permute-start.3
  24.0 2.4 collective-permute-start.2
  28.2 3.9 %collective-permute-done.2 = bf16[3,1,48,8,7]{4,2,3,0,1:T(8,128)(2,1)S(1)} collective-permute-done((bf16[3,1,48,8,7]{4,2,3,0,1:T(8,128)(2,1)S(1)}, bf16[3,1,48,8,7]{4,2,3,0,1:T(8,128)(2,1)S(1)}, u32[]{:S(2)}, u32[]{:S(2)}) %collective-permute-start.2) | collective-permute-done | bytes 16160 | tf_op jit(solution)/shard_map/ppermute | solution.py:15
  35.1 1.1 fusion.6
  36.2 0.8 reshape.645
  43.2 1.7 reshape.646
  44.9 10.0 %all-to-all-start.1 = ((bf16[32,2,2304]{2,1,0:T(2,128)(2,1)}), bf16[32,2,2304]{2,1,0:T(2,128)(2,1)S(1)}, u32[]{:S(2)}, u32[]{:S(2)}) async-start(bf16[32,2,2304]{2,1,0:T(2,128)(2,1)} %reshape.646), calls=%async_computation.1 | async-start | bytes 589824 | tf_op jit(solution)/shard_map/all_to_all | solution.py:66
  54.9 1.0 fusion.5
  55.9 1.0 fusion.4
  56.9 1.0 fusion.3
  58.5 1.7 reshape.648
  60.2 6.9 %all-to-all-done.1 = bf16[32,2,2304]{2,1,0:T(2,128)(2,1)S(1)} async-done(((bf16[32,2,2304]{2,1,0:T(2,128)(2,1)}), bf16[32,2,2304]{2,1,0:T(2,128)(2,1)S(1)}, u32[]{:S(2)}, u32[]{:S(2)}) %all-to-all-start.1) | async-done | bytes 294944 | tf_op jit(solution)/shard_map/all_to_all | solution.py:66
  67.1 4.7 %all-to-all-start.2 = ((bf16[32,2,2304]{2,1,0:T(2,128)(2,1)}), bf16[32,2,2304]{2,1,0:T(2,128)(2,1)S(1)}, u32[]{:S(2)}, u32[]{:S(2)}) async-start(bf16[32,2,2304]{2,1,0:T(2,128)(2,1)} %reshape.648), calls=%async_computation.2 | async-start | bytes 589824 | tf_op jit(solution)/shard_map/all_to_all | solution.py:67
  71.9 1.9 fusion.2
  73.7 0.8 reshape.647
  75.8 0.9 fusion.299
  76.7 1.9 collective-permute-start.1
  78.6 2.4 collective-permute-start
  81.0 1.1 fusion.178
  82.1 1.3 all-to-all-done.2
  83.4 0.8 reshape.649
  84.6 1.3 copy.202
  85.9 1.9 fusion.65
  87.9 3.8 %collective-permute-start.4 = (bf16[2,3,1,48,7,128]{5,3,4,1,2,0:T(8,128)(2,1)S(1)}, bf16[2,3,1,48,7,128]{5,3,4,1,2,0:T(8,128)(2,1)S(1)}, u32[]{:S(2)}, u32[]{:S(2)}) collective-permute-start(bf16[2,3,1,48,7,128]{5,3,4,1,2,0:T(8,128)(2,1)S(1)} %get-tuple-element.22), channel_id=1, source_target_pairs={{0,8},{8,16},{16,24},{24,32},{32,40},{40,48},{48,56},{56,64},{64,7... | collective-permute-start | bytes 1548296 | tf_op jit(solution)/shard_map/ppermute | solution.py:15
  91.7 1.5 collective-permute-start.5
  103.7 0.8 copy.220
  113.5 65.6 %all-reduce.8.cloned.1.call-done = (f32[15,48,48]{2,1,0:T(8,128)}, f32[15,48,48]{2,1,0:T(8,128)}) async-done(((f32[15,48,48]{2,1,0:T(8,128)}, f32[15,48,48]{2,1,0:T(8,128)}), (f32[15,48,48]{2,1,0:T(8,128)}, f32[15,48,48]{2,1,0:T(8,128)})) %all-reduce.8.cloned.1.call-update) | async-done | bytes 276496 | tf_op jit(solution)/shard_map/psum | solution.py:83
  180.4 152.3 %all-reduce.6.cloned.1.call-done = (f32[15,48,48]{2,1,0:T(8,128)}, f32[15,48,48]{2,1,0:T(8,128)}) async-done(((f32[15,48,48]{2,1,0:T(8,128)}, f32[15,48,48]{2,1,0:T(8,128)}), (f32[15,48,48]{2,1,0:T(8,128)}, f32[15,48,48]{2,1,0:T(8,128)})) %all-reduce.6.cloned.1.call-update) | async-done | bytes 276496 | tf_op jit(solution)/shard_map/psum | solution.py:83
  332.7 2.0 broadcast_multiply_fusion
  (145 shorter events, 33.2 us)
Async XLA Ops:
  7.2 14.7 %copy-start = (bf16[3,1,48,8,128]{4,3,2,1,0:T(8,128)(2,1)S(1)}, bf16[3,1,48,8,128]{4,3,2,1,0:T(8,128)(2,1)}, u32[]{:S(2)}) copy-start(bf16[3,1,48,8,128]{4,3,2,1,0:T(8,128)(2,1)} %param.7) | copy-start | bytes 884740
  8.8 17.7 %copy-start.9 = (bf16[15,48,48]{2,1,0:T(8,128)(2,1)S(1)}, bf16[15,48,48]{2,1,0:T(8,128)(2,1)}, u32[]{:S(2)}) copy-start(bf16[15,48,48]{2,1,0:T(8,128)(2,1)} %param.6) | copy-start | bytes 207364
  10.5 25.7 %all-to-all-start = ((bf16[32,2,2304]{2,1,0:T(2,128)(2,1)}), bf16[32,2,2304]{2,1,0:T(2,128)(2,1)S(1)}, u32[]{:S(2)}, u32[]{:S(2)}) async-start(bf16[32,2,2304]{2,1,0:T(2,128)(2,1)} %reshape.644), calls=%async_computation | async-start | bytes 589824 | tf_op jit(solution)/shard_map/all_to_all | solution.py:61
  21.8 4.9 %copy-start.8 = (bf16[15,48,48]{2,1,0:T(8,128)(2,1)S(1)}, bf16[15,48,48]{2,1,0:T(8,128)(2,1)}, u32[]{:S(2)}) copy-start(bf16[15,48,48]{2,1,0:T(8,128)(2,1)} %param.5) | copy-start | bytes 207364
  21.9 5.5 %copy-start.2 = (bf16[3,1,48,8,128]{4,3,2,1,0:T(8,128)(2,1)S(1)}, bf16[3,1,48,8,128]{4,3,2,1,0:T(8,128)(2,1)}, u32[]{:S(2)}) copy-start(bf16[3,1,48,8,128]{4,3,2,1,0:T(8,128)(2,1)} %param.4) | copy-start | bytes 884740
  22.1 12.6 %collective-permute-start.3 = (bf16[3,1,48,8,7]{4,2,3,0,1:T(8,128)(2,1)S(1)}, bf16[3,1,48,8,7]{4,2,3,0,1:T(8,128)(2,1)S(1)}, u32[]{:S(2)}, u32[]{:S(2)}) collective-permute-start(bf16[3,1,48,8,7]{4,2,3,0,1:T(8,128)(2,1)S(1)} %get-tuple-element.24), channel_id=1, source_target_pairs={{1,0},{2,1},{3,2},{4,3},{5,4},{6,5},{7,6},{9,8},{10,9},{11,10},{12... | collective-permute-start | bytes 48392 | tf_op jit(solution)/shard_map/ppermute | solution.py:17
  24.0 8.0 %collective-permute-start.2 = (bf16[3,1,48,8,7]{4,2,3,0,1:T(8,128)(2,1)S(1)}, bf16[3,1,48,8,7]{4,2,3,0,1:T(8,128)(2,1)S(1)}, u32[]{:S(2)}, u32[]{:S(2)}) collective-permute-start(bf16[3,1,48,8,7]{4,2,3,0,1:T(8,128)(2,1)S(1)} %get-tuple-element.25), channel_id=1, source_target_pairs={{0,1},{1,2},{2,3},{3,4},{4,5},{5,6},{6,7},{8,9},{9,10},{10,11},{11... | collective-permute-start | bytes 48392 | tf_op jit(solution)/shard_map/ppermute | solution.py:15
  26.5 8.6 %copy-start.12 = (bf16[15,48,48]{1,2,0:T(8,128)(2,1)}, bf16[15,48,48]{1,2,0:T(8,128)(2,1)S(1)}, u32[]{:S(2)}) copy-start(bf16[15,48,48]{1,2,0:T(8,128)(2,1)S(1)} %reverse_bitcast_fusion.1) | copy-start | bytes 207364
  42.4 12.5 %copy-start.5 = (f32[48,3,8,128]{3,0,2,1:T(8,128)S(1)}, f32[48,3,8,128]{3,0,2,1:T(8,128)}, u32[]{:S(2)}) copy-start(f32[48,3,8,128]{3,0,2,1:T(8,128)} %fusion.6) | copy-start | bytes 1769476
  44.9 22.2 %all-to-all-start.1 = ((bf16[32,2,2304]{2,1,0:T(2,128)(2,1)}), bf16[32,2,2304]{2,1,0:T(2,128)(2,1)S(1)}, u32[]{:S(2)}, u32[]{:S(2)}) async-start(bf16[32,2,2304]{2,1,0:T(2,128)(2,1)} %reshape.646), calls=%async_computation.1 | async-start | bytes 589824 | tf_op jit(solution)/shard_map/all_to_all | solution.py:66
  67.1 16.3 %all-to-all-start.2 = ((bf16[32,2,2304]{2,1,0:T(2,128)(2,1)}), bf16[32,2,2304]{2,1,0:T(2,128)(2,1)S(1)}, u32[]{:S(2)}, u32[]{:S(2)}) async-start(bf16[32,2,2304]{2,1,0:T(2,128)(2,1)} %reshape.648), calls=%async_computation.2 | async-start | bytes 589824 | tf_op jit(solution)/shard_map/all_to_all | solution.py:67
  71.8 107.3 %all-reduce.8.cloned.1.call-start = ((), (), s32[]{:S(2)}) async-start(), calls=%async_computation.4 | async-start | bytes 1474560 | tf_op jit(solution)/shard_map/psum | solution.py:83
  74.8 6.2 %copy-start.10 = (bf16[15,48,48]{2,1,0:T(8,128)(2,1)S(1)}, bf16[15,48,48]{2,1,0:T(8,128)(2,1)}, u32[]{:S(2)}) copy-start(bf16[15,48,48]{2,1,0:T(8,128)(2,1)} %param.6) | copy-start | bytes 207364
  75.8 8.4 %copy-start.6 = (bf16[3,48,8,128]{3,1,2,0:T(8,128)(2,1)}, bf16[3,48,8,128]{3,1,2,0:T(8,128)(2,1)S(1)}, u32[]{:S(2)}) copy-start(bf16[3,48,8,128]{3,1,2,0:T(8,128)(2,1)S(1)} %copy.179) | copy-start | bytes 884740
  76.7 19.7 %collective-permute-start.1 = (bf16[3,1,48,8,7]{4,2,3,0,1:T(8,128)(2,1)}, bf16[3,1,48,8,7]{4,2,3,0,1:T(8,128)(2,1)S(1)}, u32[]{:S(2)}, u32[]{:S(2)}) collective-permute-start(bf16[3,1,48,8,7]{4,2,3,0,1:T(8,128)(2,1)} %get-tuple-element.28), channel_id=1, source_target_pairs={{1,0},{2,1},{3,2},{4,3},{5,4},{6,5},{7,6},{9,8},{10,9},{11,10},{12... | collective-permute-start | bytes 48392 | tf_op jit(solution)/shard_map/ppermute | solution.py:17
  78.6 14.6 %collective-permute-start = (bf16[3,1,48,8,7]{4,2,3,0,1:T(8,128)(2,1)}, bf16[3,1,48,8,7]{4,2,3,0,1:T(8,128)(2,1)S(1)}, u32[]{:S(2)}, u32[]{:S(2)}) collective-permute-start(bf16[3,1,48,8,7]{4,2,3,0,1:T(8,128)(2,1)} %get-tuple-element.29), channel_id=1, source_target_pairs={{0,1},{1,2},{2,3},{3,4},{4,5},{5,6},{6,7},{8,9},{9,10},{10,11},{11... | collective-permute-start | bytes 48392 | tf_op jit(solution)/shard_map/ppermute | solution.py:15
  85.9 1.9 copy-start.1
  87.9 17.3 %collective-permute-start.4 = (bf16[2,3,1,48,7,128]{5,3,4,1,2,0:T(8,128)(2,1)S(1)}, bf16[2,3,1,48,7,128]{5,3,4,1,2,0:T(8,128)(2,1)S(1)}, u32[]{:S(2)}, u32[]{:S(2)}) collective-permute-start(bf16[2,3,1,48,7,128]{5,3,4,1,2,0:T(8,128)(2,1)S(1)} %get-tuple-element.22), channel_id=1, source_target_pairs={{0,8},{8,16},{16,24},{24,32},{32,40},{40,48},{48,56},{56,64},{64,7... | collective-permute-start | bytes 1548296 | tf_op jit(solution)/shard_map/ppermute | solution.py:15
  91.7 14.8 %collective-permute-start.5 = (bf16[2,3,1,48,7,128]{5,3,4,1,2,0:T(8,128)(2,1)S(1)}, bf16[2,3,1,48,7,128]{5,3,4,1,2,0:T(8,128)(2,1)S(1)}, u32[]{:S(2)}, u32[]{:S(2)}) collective-permute-start(bf16[2,3,1,48,7,128]{5,3,4,1,2,0:T(8,128)(2,1)S(1)} %get-tuple-element.23), channel_id=1, source_target_pairs={{8,0},{16,8},{24,16},{32,24},{40,32},{48,40},{56,48},{64,56},{72,6... | collective-permute-start | bytes 1548296 | tf_op jit(solution)/shard_map/ppermute | solution.py:17
  94.6 1.1 copy-start.7
  98.9 1.1 copy-start.4
  102.0 1.0 copy-start.3
  105.2 0.7 copy-start.13
  109.3 1.2 copy-start.11
  110.5 0.7 copy-start.14
  113.2 219.5 %all-reduce.6.cloned.1.call-start = ((), (), s32[]{:S(2)}) async-start(), calls=%async_computation.3 | async-start | bytes 1474560 | tf_op jit(solution)/shard_map/psum | solution.py:83
Sparse Core Ops, SparseCore 0:
  113.3 65.7 all-reduce.7
  182.9 149.7 all-reduce.5
